TPU v7x, 128 devices: a whole 4x4x4 slice. The times are simulated.
128 devices in a mesh: seq: 64 (over z, x, y_lo, core), chan: 2 (over y_hi).
Axes of the slice: x: 4, y: 4 (y_hi: 2, y_lo: 2; y = y_hi * 2 + y_lo), z: 4, core: 2. Of those that a mesh axis runs over, the one named last changes fastest.
Arguments:
- signal: bfloat16 [2, 32768, 128], P('chan', 'seq'), may hold values from -6 to 6
- cotangent: bfloat16 [2, 32768, 128], P('chan', 'seq'), may hold values from -6 to 6
- band_freq: int32 [16], replicated, may hold values from 1 to 8191
- w_embed: float32 [32, 64], replicated, may hold values from -2 to 2
- b_embed: float32 [64], replicated, may hold values from -3.140625 to 3.140625
- w_out: float32 [64, 128], P(None, 'chan'), may hold values from -0.75 to 0.75
- decay: float32 [128], P('chan'), may hold values from 0.25 to 16, as said below
Outputs:
- conv_out: bfloat16 [2, 32768, 128], P('chan', 'seq')
- d_signal: bfloat16 [2, 32768, 128], P('chan', 'seq')
- grad_embed: float32 [32, 64], replicated
- grad_bias: float32 [64], replicated
- grad_out: float32 [64, 128], P(None, 'chan')
Inputs may be any that keep to these rules, and one draw needn't show every extreme that they name: decay rates are positive.
All inputs are finite; a program needn't handle non-finite values.
Results may differ from a plain program's by a relative error of at most 0.007.
Values may be sent and summed in bfloat16 or wider, within the bound.
No kernel may reach another device: no remote copies, remote signals or barrier semaphores. Data moves between devices by JAX's collectives and lax.ppermute only.
A program may use at most 192 MiB of HBM per device.

v0:
```python
import math

import jax
import jax.numpy as jnp
from jax import lax
from jax.sharding import PartitionSpec as P

exact_mode = lax.Precision.HIGHEST


def mat_dot(lhs_mat, rhs_mat):
    return jnp.dot(lhs_mat, rhs_mat, preferred_element_type=jnp.float32, precision=exact_mode)


def side_dot(table, values):
    return jnp.einsum(
        "db,cbm->cdm", table, values, preferred_element_type=jnp.float32, precision=exact_mode
    )


def inner_dot(table, values):
    return jnp.einsum(
        "eb,cdbh->cdeh", table, values, preferred_element_type=jnp.float32, precision=exact_mode
    )


def band_phase(band_freq, places, seq_total):
    upper_part = places // 1024
    lower_part = places % 1024
    partial_turn = upper_part[:, None] * band_freq[None, :] % seq_total
    wrapped = (partial_turn * 1024 + lower_part[:, None] * band_freq[None, :]) % seq_total
    return wrapped.astype(jnp.float32) * (2.0 * math.pi / seq_total)


def filter_parts(places, band_freq, w_embed, b_embed, w_out, decay, seq_total):
    phases = band_phase(band_freq, places, seq_total)
    features = jnp.concatenate([jnp.cos(phases), jnp.sin(phases)], axis=1)
    preact = mat_dot(features, w_embed) + b_embed[None, :]
    hidden = jnp.sin(preact)
    fraction = places.astype(jnp.float32) / seq_total
    envelope = (
        jnp.exp(-decay[None, :] * fraction[:, None]) * jnp.sqrt((1.0 + decay) / seq_total)[None, :]
    )
    taps = mat_dot(hidden, w_out) * envelope
    return (features, preact, hidden, taps, envelope)


def angle_table(rows_idx, cols_idx, modulus):
    wrapped = rows_idx[:, None] * cols_idx[None, :] % modulus
    angles = wrapped.astype(jnp.float32) * (2.0 * math.pi / modulus)
    return (jnp.cos(angles), jnp.sin(angles))


def local(signal, cotangent, band_freq, w_embed, b_embed, w_out, decay):
    devices = lax.axis_size("seq")
    rank_seq = lax.axis_index("seq")
    seg_len = signal.shape[1] * 2
    channels = signal.shape[2] // 2
    block_w = seg_len // devices
    rows_all = 2 * devices
    seq_total = seg_len * devices
    fft_size = 2 * seq_total
    inv_scale = 1.0 / fft_size
    radix_one = max(
        (divisor for divisor in range(1, math.isqrt(seg_len) + 1) if seg_len % divisor == 0)
    )
    radix_two = seg_len // radix_one
    row_ids = jnp.arange(rows_all, dtype=jnp.int32)
    src_ids = jnp.arange(devices, dtype=jnp.int32)
    col_glob = rank_seq * block_w + jnp.arange(block_w, dtype=jnp.int32)
    seg_ids = jnp.arange(seg_len, dtype=jnp.int32)
    one_ids = jnp.arange(radix_one, dtype=jnp.int32)
    two_ids = jnp.arange(radix_two, dtype=jnp.int32)
    pair_ids = lax.dynamic_slice_in_dim(row_ids, 2 * rank_seq, 2)
    outer_cos, outer_sin = angle_table(row_ids, src_ids, rows_all)
    entry_cos, entry_sin = angle_table(row_ids, col_glob, fft_size)
    first_cos, first_sin = angle_table(one_ids, one_ids, radix_one)
    second_cos, second_sin = angle_table(two_ids, two_ids, radix_two)
    inner_cos, inner_sin = angle_table(one_ids, two_ids, seg_len)
    exit_cos, exit_sin = angle_table(pair_ids, seg_ids, fft_size)
    inner_c = inner_cos[None, :, :, None]
    inner_s = inner_sin[None, :, :, None]

    def twist_stack(real_a, imag_a):
        real_a = real_a.reshape(rows_all, block_w, channels)
        imag_a = imag_a.reshape(rows_all, block_w, channels)
        twist_c = entry_cos[:, :, None]
        twist_s = entry_sin[:, :, None]
        real_b = real_a * twist_c + imag_a * twist_s
        imag_b = imag_a * twist_c - real_a * twist_s
        return jnp.stack([real_b, imag_b]).reshape(2, rows_all, block_w * channels)

    def column_pass(cols_data):
        return twist_stack(mat_dot(outer_cos, cols_data), -mat_dot(outer_sin, cols_data))

    def local_forward(stacked):
        grid = stacked.reshape(2, 2, radix_one, radix_two * channels)
        part_r = side_dot(first_cos, grid[0]) + side_dot(first_sin, grid[1])
        part_i = side_dot(first_cos, grid[1]) - side_dot(first_sin, grid[0])
        part_r = part_r.reshape(2, radix_one, radix_two, channels)
        part_i = part_i.reshape(2, radix_one, radix_two, channels)
        turn_r = part_r * inner_c + part_i * inner_s
        turn_i = part_i * inner_c - part_r * inner_s
        spec_r = inner_dot(second_cos, turn_r) + inner_dot(second_sin, turn_i)
        spec_i = inner_dot(second_cos, turn_i) - inner_dot(second_sin, turn_r)
        return (spec_r, spec_i)

    def local_inverse(spec_r, spec_i):
        back_r = inner_dot(second_cos, spec_r) - inner_dot(second_sin, spec_i)
        back_i = inner_dot(second_cos, spec_i) + inner_dot(second_sin, spec_r)
        turn_r = (back_r * inner_c - back_i * inner_s).reshape(2, radix_one, radix_two * channels)
        turn_i = (back_r * inner_s + back_i * inner_c).reshape(2, radix_one, radix_two * channels)
        time_r = (side_dot(first_cos, turn_r) - side_dot(first_sin, turn_i)).reshape(
            2, seg_len, channels
        )
        time_i = (side_dot(first_cos, turn_i) + side_dot(first_sin, turn_r)).reshape(
            2, seg_len, channels
        )
        twist_c = exit_cos[:, :, None]
        twist_s = exit_sin[:, :, None]
        final_r = time_r * twist_c - time_i * twist_s
        final_i = time_r * twist_s + time_i * twist_c
        return jnp.stack([final_r, final_i]).reshape(2, 2, seg_len * channels)

    def real_rows(gathered):
        return mat_dot(outer_cos.T, gathered[0]) - mat_dot(outer_sin.T, gathered[1])

    sig_cols, cot_cols = (
        lax.all_to_all(
            signal.reshape(devices, block_w * channels),
            "seq",
            split_axis=0,
            concat_axis=0,
            tiled=True,
        ),
        lax.all_to_all(
            cotangent.reshape(devices, block_w * channels),
            "seq",
            split_axis=0,
            concat_axis=0,
            tiled=True,
        ),
    )
    places = rank_seq * seg_len + seg_ids
    features, preact, hidden, taps, envelope = filter_parts(
        places, band_freq, w_embed, b_embed, w_out, decay, seq_total
    )
    tap_cols = lax.all_to_all(
        taps.reshape(devices, block_w * channels), "seq", split_axis=0, concat_axis=0, tiled=True
    )
    spec_sig, spec_cot, spec_tap = (
        lax.all_to_all(
            column_pass(sig_cols.astype(jnp.float32)),
            "seq",
            split_axis=1,
            concat_axis=2,
            tiled=True,
        ),
        lax.all_to_all(
            column_pass(cot_cols.astype(jnp.float32)),
            "seq",
            split_axis=1,
            concat_axis=2,
            tiled=True,
        ),
        lax.all_to_all(column_pass(tap_cols), "seq", split_axis=1, concat_axis=2, tiled=True),
    )
    sig_r, sig_i = local_forward(spec_sig)
    cot_r, cot_i = local_forward(spec_cot)
    tap_r, tap_i = local_forward(spec_tap)
    prod_r = sig_r * tap_r - sig_i * tap_i
    prod_i = sig_r * tap_i + sig_i * tap_r
    grad_r = cot_r * tap_r + cot_i * tap_i
    grad_i = cot_i * tap_r - cot_r * tap_i
    corr_r = cot_r * sig_r + cot_i * sig_i
    corr_i = cot_i * sig_r - cot_r * sig_i
    prod_back, grad_back, corr_back = (
        lax.all_to_all(
            local_inverse(prod_r, prod_i), "seq", split_axis=2, concat_axis=1, tiled=True
        ),
        lax.all_to_all(
            local_inverse(grad_r, grad_i), "seq", split_axis=2, concat_axis=1, tiled=True
        ),
        lax.all_to_all(
            local_inverse(corr_r, corr_i), "seq", split_axis=2, concat_axis=1, tiled=True
        ),
    )
    out_cols = real_rows(prod_back)
    dsig_cols = real_rows(grad_back)
    dtap_cols = real_rows(corr_back) * inv_scale
    out_rows, dsig_rows = (
        lax.all_to_all(
            (out_cols * inv_scale).astype(jnp.bfloat16),
            "seq",
            split_axis=0,
            concat_axis=0,
            tiled=True,
        ),
        lax.all_to_all(
            (dsig_cols * inv_scale).astype(jnp.bfloat16),
            "seq",
            split_axis=0,
            concat_axis=0,
            tiled=True,
        ),
    )
    conv_out = out_rows.reshape(1, seg_len // 2, 2 * channels)
    d_signal = dsig_rows.reshape(1, seg_len // 2, 2 * channels)
    d_taps = (
        lax.all_to_all(
            dtap_cols.astype(jnp.bfloat16), "seq", split_axis=0, concat_axis=0, tiled=True
        )
        .astype(dtap_cols.dtype)
        .reshape(seg_len, channels)
    )
    d_raw = d_taps * envelope
    d_preact = mat_dot(d_raw, w_out.T) * jnp.cos(preact)
    out_part = mat_dot(hidden.T, d_raw)
    embed_part = mat_dot(features.T, d_preact)
    bias_part = jnp.sum(d_preact, axis=0)
    out_sum, embed_sum, bias_sum = lax.psum((out_part, embed_part, bias_part), "seq")
    embed_all, bias_all = lax.psum((embed_sum, bias_sum), "chan")
    norm_scale = 1.0 / math.sqrt(seq_total)
    return (conv_out, d_signal, embed_all * norm_scale, bias_all * norm_scale, out_sum * norm_scale)


def solution(mesh):
    return jax.shard_map(
        local,
        mesh=mesh,
        in_specs=(
            P("chan", "seq", None),
            P("chan", "seq", None),
            P(),
            P(),
            P(),
            P(None, "chan"),
            P("chan"),
        ),
        out_specs=(P("chan", "seq", None), P("chan", "seq", None), P(), P(), P(None, "chan")),
        check_vma=False,
    )
```

profile of v0, /device:TPU:0, one launch (start us, length us, event | category | flops | bytes accessed | tf_op | source)
XLA Modules:
  0.0 1673.4 jit_solution(10459679201133411678)
XLA Ops:
  4.5 9.9 all-to-all-start
  19.5 2.7 fusion.489
  24.7 8.8 all-to-all-start.6
  34.2 7.9 all-to-all-done.6
  42.1 5.1 all-to-all-start.2
  49.2 7.9 all-to-all-done.2
  59.8 3.0 multiply_add_fusion.8
  65.5 1.9 pad_maximum_fusion.1
  67.4 4.7 all-to-all-start.3
  79.9 2.0 pad_maximum_fusion.3
  81.9 3.0 pad_maximum_fusion
  84.9 5.3 all-to-all-done.3
  90.2 4.7 all-to-all-start.1
  94.9 1.6 fusion.486
  101.8 11.2 all-to-all-done.1
  113.0 5.7 all-to-all-start.7
  123.7 2.3 fusion.40
  126.0 2.5 fusion.3
  129.9 2.8 reshape.612
  132.7 2.3 fusion.39
  135.0 3.5 fusion.42
  138.5 3.5 fusion.41
  142.0 3.8 fusion.484
  146.8 2.0 squeeze.48
  148.9 2.5 fusion.132
  151.4 2.0 copy.97
  153.4 2.0 squeeze.49
  155.5 1.7 fusion.130
  157.2 2.7 fusion.6
  159.9 2.5 fusion.7
  167.9 2.8 convolution_subtract_fusion.11
  170.7 2.8 convolution_add_fusion.11
  173.6 3.1 convolution_subtract_fusion.10
  176.7 3.6 convolution_add_fusion.10
  181.6 1.9 multiply_add_fusion
  195.8 3.3 subtract_bitcast_fusion
  222.6 1.9 reshape.630
  224.5 3.6 multiply_subtract_fusion.6
  228.6 58.0 %copy.88 = f32[2,2,65536]{1,0,2:T(2,128)} copy(f32[2,2,65536]{2,1,0:T(2,128)S(1)} %pad_maximum_fusion.2) | data formatting | bytes 2097152 | tf_op jit(solution)/shard_map/stack | solution.py:123
  286.6 96.8 %reshape.642 = f32[64,1,4096]{2,1,0:T(1,128)} reshape(f32[65536,2,2]{2,1,0:T(2,128)} %bitcast.255) | data formatting | bytes 2097152
  383.4 8.7 all-to-all-start.4
  392.7 58.0 %copy.98 = f32[2,2,65536]{1,0,2:T(2,128)} copy(f32[2,2,65536]{2,1,0:T(2,128)S(1)} %pad_maximum_fusion.4) | data formatting | bytes 2097152 | tf_op jit(solution)/shard_map/stack | solution.py:123
  450.7 96.8 %reshape.648 = f32[64,1,4096]{2,1,0:T(1,128)} reshape(f32[65536,2,2]{2,1,0:T(2,128)} %bitcast.257) | data formatting | bytes 2097152
  547.5 8.8 all-to-all-start.8
  556.3 1.7 pad_maximum_fusion.5
  558.0 58.0 %copy.101 = f32[2,2,65536]{1,0,2:T(2,128)} copy(f32[2,2,65536]{2,1,0:T(2,128)S(1)} %pad_maximum_fusion.5) | data formatting | bytes 2097152 | tf_op jit(solution)/shard_map/stack | solution.py:123
  616.0 96.8 %reshape.652 = f32[64,1,4096]{2,1,0:T(1,128)} reshape(f32[65536,2,2]{2,1,0:T(2,128)} %bitcast.259) | data formatting | bytes 2097152
  713.3 3.3 reduce.6
  716.5 129.2 %reshape.643 = f32[65536,2,2]{2,1,0:T(2,128)} reshape(f32[64,4096]{1,0:T(8,128)S(1)} %reduce.6) | data formatting | bytes 2097152
  845.8 71.0 %copy.89 = f32[2,2,64,1024]{3,1,2,0:T(2,128)S(1)} copy(f32[2,2,64,1024]{1,0,3,2:T(2,128)} %bitcast.35) | data formatting | bytes 2097152 | tf_op jit(solution)/shard_map/all_to_all | solution.py:178
  917.6 9.1 all-to-all-start.10
  929.1 3.3 reduce.8
  932.4 129.0 %reshape.649 = f32[65536,2,2]{2,1,0:T(2,128)} reshape(f32[64,4096]{1,0:T(8,128)S(1)} %reduce.8) | data formatting | bytes 2097152
  1061.4 71.0 %copy.99 = f32[2,2,64,1024]{3,1,2,0:T(2,128)S(1)} copy(f32[2,2,64,1024]{1,0,3,2:T(2,128)} %bitcast.54) | data formatting | bytes 2097152 | tf_op jit(solution)/shard_map/all_to_all | solution.py:181
  1135.7 9.4 all-to-all-start.5
  1145.1 3.3 reduce.10
  1148.4 129.0 %reshape.653 = f32[65536,2,2]{2,1,0:T(2,128)} reshape(f32[64,4096]{1,0:T(8,128)S(1)} %reduce.10) | data formatting | bytes 2097152
  1277.5 71.0 %copy.102 = f32[2,2,64,1024]{3,1,2,0:T(2,128)S(1)} copy(f32[2,2,64,1024]{1,0,3,2:T(2,128)} %bitcast.63) | data formatting | bytes 2097152 | tf_op jit(solution)/shard_map/all_to_all | solution.py:184
  1349.8 9.1 all-to-all-start.9
  1360.9 6.4 all-to-all-done.9
  1367.4 4.6 all-to-all-start.11
  1375.1 5.4 all-to-all-done.11
  1383.9 276.3 %all-reduce = (f32[32,64]{1,0:T(8,128)S(1)}, f32[64]{0:T(128)S(1)}, f32[64,64]{1,0:T(8,128)S(1)}) all-reduce(f32[32,64]{1,0:T(8,128)S(1)} %fusion.61, f32[64]{0:T(128)S(1)} %get-tuple-element.72, f32[64,64]{1,0:T(8,128)S(1)} %fusion.48), channel_id=1, replica_groups=mesh['seq'=64,'chan'=2] {'seq'}, use_global_device_ids=true, to_apply=%region_0.1 | all-reduce | flops 6208 | bytes 49664 | tf_op jit(solution)/shard_map/psum | solution.py:221
  1660.2 11.2 all-reduce.1
  (184 shorter events, 101.6 us)
Async XLA Ops:
  0.6 22.3 %copy-start = (f32[64,64]{1,0:T(8,128)S(1)}, f32[64,64]{1,0:T(8,128)}, u32[]{:S(2)}) copy-start(f32[64,64]{1,0:T(8,128)} %param.12) | copy-start | bytes 49156
  4.5 20.2 %all-to-all-start = ((bf16[64,2,512]{2,1,0:T(2,128)(2,1)}), bf16[64,2,512]{2,1,0:T(2,128)(2,1)S(1)}, u32[]{:S(2)}, u32[]{:S(2)}) async-start(bf16[64,2,512]{2,1,0:T(2,128)(2,1)} %reshape.640), calls=%async_computation | async-start | bytes 262144 | tf_op jit(solution)/shard_map/all_to_all | solution.py:129
  14.4 7.8 copy-start.12
  15.1 7.1 copy-start.14
  15.1 7.1 copy-start.16
  19.5 2.7 copy-start.8
  19.5 2.7 copy-start.10
  22.2 0.7 copy-start.3
  24.7 17.4 %all-to-all-start.6 = ((bf16[64,2,512]{2,1,0:T(2,128)(2,1)}), bf16[64,2,512]{2,1,0:T(2,128)(2,1)S(1)}, u32[]{:S(2)}, u32[]{:S(2)}) async-start(bf16[64,2,512]{2,1,0:T(2,128)(2,1)} %reshape.646), calls=%async_computation.6 | async-start | bytes 262144 | tf_op jit(solution)/shard_map/all_to_all | solution.py:136
  42.1 15.0 all-to-all-start.2
  67.4 22.7 %all-to-all-start.3 = ((f32[2,128,1024]{2,0,1:T(2,128)}), f32[2,128,1024]{2,0,1:T(2,128)S(1)}, u32[]{:S(2)}, u32[]{:S(2)}) async-start(f32[2,128,1024]{2,0,1:T(2,128)} %pad_maximum_fusion.1), calls=%async_computation.3 | async-start | bytes 2097152 | tf_op jit(solution)/shard_map/all_to_all | solution.py:166
  90.2 22.8 %all-to-all-start.1 = ((f32[2,128,1024]{2,0,1:T(2,128)}), f32[2,128,1024]{2,0,1:T(2,128)S(1)}, u32[]{:S(2)}, u32[]{:S(2)}) async-start(f32[2,128,1024]{2,0,1:T(2,128)} %pad_maximum_fusion), calls=%async_computation.1 | async-start | bytes 2097152 | tf_op jit(solution)/shard_map/all_to_all | solution.py:152
  113.0 29.0 %all-to-all-start.7 = ((f32[2,128,1024]{2,0,1:T(2,128)}), f32[2,128,1024]{2,0,1:T(2,128)}, u32[]{:S(2)}, u32[]{:S(2)}) async-start(f32[2,128,1024]{2,0,1:T(2,128)} %pad_maximum_fusion.3), calls=%async_computation.7 | async-start | bytes 2097152 | tf_op jit(solution)/shard_map/all_to_all | solution.py:159
  123.7 36.2 %copy-start.1 = (f32[2,32,32,64]{3,2,1,0:T(8,128)}, f32[2,32,32,64]{3,2,1,0:T(8,128)S(1)}, u32[]{:S(2)}) copy-start(f32[2,32,32,64]{3,2,1,0:T(8,128)S(1)} %reshape.610) | copy-start | bytes 1572868
  129.9 32.5 %copy-start.2 = (f32[2,32,32,64]{3,2,1,0:T(8,128)}, f32[2,32,32,64]{3,2,1,0:T(8,128)S(1)}, u32[]{:S(2)}) copy-start(f32[2,32,32,64]{3,2,1,0:T(8,128)S(1)} %reshape.613) | copy-start | bytes 1572868
  228.6 163.6 %copy-start.5 = (f32[1,2,65536]{2,1,0:T(2,128)S(1)}, f32[1,2,65536]{2,1,0:T(2,128)}, u32[]{:S(2)}) copy-start(f32[1,2,65536]{2,1,0:T(2,128)} %get-tuple-element.40) | copy-start | bytes 1572868
  228.6 163.6 %copy-start.6 = (f32[1,2,65536]{2,1,0:T(2,128)S(1)}, f32[1,2,65536]{2,1,0:T(2,128)}, u32[]{:S(2)}) copy-start(f32[1,2,65536]{2,1,0:T(2,128)} %get-tuple-element.41) | copy-start | bytes 1572868
  383.4 164.0 %all-to-all-start.4 = ((f32[64,1,4096]{2,1,0:T(1,128)}), f32[64,1,4096]{2,1,0:T(1,128)S(1)}, u32[]{:S(2)}, u32[]{:S(2)}) async-start(f32[64,1,4096]{2,1,0:T(1,128)} %reshape.642), calls=%async_computation.4 | async-start | bytes 2097152 | tf_op jit(solution)/shard_map/all_to_all | solution.py:178
  547.5 370.1 %all-to-all-start.8 = ((f32[64,1,4096]{2,1,0:T(1,128)}), f32[64,1,4096]{2,1,0:T(1,128)S(1)}, u32[]{:S(2)}, u32[]{:S(2)}) async-start(f32[64,1,4096]{2,1,0:T(1,128)} %reshape.648), calls=%async_computation.8 | async-start | bytes 2097152 | tf_op jit(solution)/shard_map/all_to_all | solution.py:181
  917.6 218.2 %all-to-all-start.10 = ((f32[64,1,4096]{2,1,0:T(1,128)}), f32[64,1,4096]{2,1,0:T(1,128)S(1)}, u32[]{:S(2)}, u32[]{:S(2)}) async-start(f32[64,1,4096]{2,1,0:T(1,128)} %reshape.652), calls=%async_computation.10 | async-start | bytes 2097152 | tf_op jit(solution)/shard_map/all_to_all | solution.py:184
  1135.7 214.1 %all-to-all-start.5 = ((bf16[64,2,512]{2,1,0:T(2,128)(2,1)}), bf16[64,2,512]{2,1,0:T(2,128)(2,1)S(1)}, u32[]{:S(2)}, u32[]{:S(2)}) async-start(bf16[64,2,512]{2,1,0:T(2,128)(2,1)} %reshape.644), calls=%async_computation.5 | async-start | bytes 262144 | tf_op jit(solution)/shard_map/all_to_all | solution.py:192
  1148.4 233.3 %copy-start.4 = (f32[1024,64]{0,1:T(8,128)S(1)}, f32[1024,64]{0,1:T(8,128)}, u32[]{:S(2)}) copy-start(f32[1024,64]{0,1:T(8,128)} %copy-done.3) | copy-start | bytes 786436
  1148.4 233.3 %copy-start.13 = (f32[1024]{0:T(1024)S(1)}, f32[1024]{0:T(1024)}, u32[]{:S(2)}) copy-start(f32[1024]{0:T(1024)} %copy-done.12) | copy-start | bytes 12292
  1148.4 233.3 %copy-start.15 = (f32[64]{0:T(128)S(1)}, f32[64]{0:T(128)}, u32[]{:S(2)}) copy-start(f32[64]{0:T(128)} %copy-done.14) | copy-start | bytes 772
  1148.4 233.3 %copy-start.17 = (f32[64]{0:T(128)S(1)}, f32[64]{0:T(128)}, u32[]{:S(2)}) copy-start(f32[64]{0:T(128)} %copy-done.16) | copy-start | bytes 772
  1148.4 233.8 %copy-start.7 = (f32[1024,64]{0,1:T(8,128)S(1)}, f32[1024,64]{0,1:T(8,128)}, u32[]{:S(2)}) copy-start(f32[1024,64]{0,1:T(8,128)} %get-tuple-element.71) | copy-start | bytes 786436
  1148.4 235.1 %copy-start.9 = (f32[1024,16]{0,1:T(8,128)S(1)}, f32[1024,16]{0,1:T(8,128)}, u32[]{:S(2)}) copy-start(f32[1024,16]{0,1:T(8,128)} %copy-done.8) | copy-start | bytes 196612
  1148.4 235.1 %copy-start.11 = (f32[1024,16]{0,1:T(8,128)S(1)}, f32[1024,16]{0,1:T(8,128)}, u32[]{:S(2)}) copy-start(f32[1024,16]{0,1:T(8,128)} %copy-done.10) | copy-start | bytes 196612
  1349.8 17.5 %all-to-all-start.9 = ((bf16[64,2,512]{2,1,0:T(2,128)(2,1)}), bf16[64,2,512]{2,1,0:T(2,128)(2,1)S(1)}, u32[]{:S(2)}, u32[]{:S(2)}) async-start(bf16[64,2,512]{2,1,0:T(2,128)(2,1)} %reshape.650), calls=%async_computation.9 | async-start | bytes 262144 | tf_op jit(solution)/shard_map/all_to_all | solution.py:199
  1367.4 13.2 all-to-all-start.11
where the time goes:
time: 1690 us; the launch traced here: 1670 us
  local copies, waits for them, and re-layouts  1130 us (67%)
  blocking collectives  288 us (17%)
  matrix products  88.8 us (5%)
  starting transfers between devices  88.6 us (5%)
  waiting for transfers between devices  44.2 us (3%)
  other arithmetic  33.8 us (2%)
    unnamed x52, local copies, waits for them, and re-layouts  683 us
    psum x1, blocking collectives, local(): lax.psum((out_part, embed_part, bias_part), 'seq')  276 us
    another operation x3, local copies, waits for them, and re-layouts, local_inverse(): return jnp.stack([final_r, final_i]).reshape(2, 2, seg_len * channels)  174 us
    all_to_all x2, local copies, waits for them, and re-layouts, local(): lax.all_to_all(local_inverse(prod_r, prod_i), 'seq', split_axis=2, concat...  71.5 us
    all_to_all x1, local copies, waits for them, and re-layouts, local(): lax.all_to_all(local_inverse(corr_r, corr_i), 'seq', split_axis=2, concat...  71 us
    all_to_all x1, local copies, waits for them, and re-layouts, local(): lax.all_to_all(local_inverse(grad_r, grad_i), 'seq', split_axis=2, concat...  71 us
    dot_general x24, matrix products, inner_dot(): jnp.einsum('eb,cdbh->cdeh', table, values, preferred_element_type=jnp.flo...  45 us
  transfers between devices with their start and end apart: 12, of which 6 were waited for; matrix products, arithmetic and copies ran while one was open for 59% of the time, Pallas kernels for 0%

commit v1 on v0

v1 whole, which is shorter than its diff:
```python
import math

import jax
import jax.numpy as jnp
from jax import lax
from jax.sharding import PartitionSpec as P

exact_mode = lax.Precision.HIGHEST


def mat_dot(lhs_mat, rhs_mat):
    return jnp.dot(lhs_mat, rhs_mat, preferred_element_type=jnp.float32, precision=exact_mode)


def band_phase(band_freq, places, seq_total):
    upper_part = places // 1024
    lower_part = places % 1024
    partial_turn = upper_part[:, None] * band_freq[None, :] % seq_total
    wrapped = (partial_turn * 1024 + lower_part[:, None] * band_freq[None, :]) % seq_total
    return wrapped.astype(jnp.float32) * (2.0 * math.pi / seq_total)


def filter_parts(places, band_freq, w_embed, b_embed, w_out, decay, seq_total):
    phases = band_phase(band_freq, places, seq_total)
    features = jnp.concatenate([jnp.cos(phases), jnp.sin(phases)], axis=1)
    preact = mat_dot(features, w_embed) + b_embed[None, :]
    hidden = jnp.sin(preact)
    fraction = places.astype(jnp.float32) / seq_total
    envelope = (
        jnp.exp(-decay[None, :] * fraction[:, None]) * jnp.sqrt((1.0 + decay) / seq_total)[None, :]
    )
    taps = mat_dot(hidden, w_out) * envelope
    return (features, preact, hidden, taps, envelope)


def angle_table(rows_idx, cols_idx, modulus):
    wrapped = rows_idx[:, None] * cols_idx[None, :] % modulus
    angles = wrapped.astype(jnp.float32) * (2.0 * math.pi / modulus)
    return (jnp.cos(angles), jnp.sin(angles))


def local(signal, cotangent, band_freq, w_embed, b_embed, w_out, decay):
    devices = lax.axis_size("seq")
    rank_seq = lax.axis_index("seq")
    seg_len = signal.shape[1] * 2
    channels = signal.shape[2] // 2
    block_w = seg_len // devices
    width = block_w * channels
    rows_all = 2 * devices
    pair = rows_all // devices
    seq_total = seg_len * devices
    fft_size = 2 * seq_total
    inv_scale = 1.0 / fft_size
    n_arr = 3

    dev_ids = jnp.arange(devices, dtype=jnp.int32)
    row_ids = jnp.arange(rows_all, dtype=jnp.int32)
    blk_ids = jnp.arange(block_w, dtype=jnp.int32)
    lane_blk = jnp.arange(width, dtype=jnp.int32) // channels
    b_lane = rank_seq * block_w + lane_blk

    src = jnp.stack(
        [signal.reshape(devices, width), cotangent.reshape(devices, width)], axis=1
    )
    cols = lax.all_to_all(src, "seq", split_axis=0, concat_axis=0, tiled=True)

    places = (
        dev_ids[:, None] * seg_len + rank_seq * block_w + blk_ids[None, :]
    ).reshape(-1)
    features, preact, hidden, taps, envelope = filter_parts(
        places, band_freq, w_embed, b_embed, w_out, decay, seq_total
    )
    stacked = jnp.concatenate(
        [cols.astype(jnp.float32), taps.reshape(devices, 1, width)], axis=1
    ).reshape(devices, n_arr * width)

    col_cos, col_sin = angle_table(row_ids, dev_ids, rows_all)
    y_re = mat_dot(col_cos, stacked).reshape(rows_all, n_arr, width)
    y_im = -mat_dot(col_sin, stacked).reshape(rows_all, n_arr, width)
    tw_cos, tw_sin = angle_table(row_ids, b_lane, fft_size)
    tw_cos = tw_cos[:, None, :]
    tw_sin = tw_sin[:, None, :]
    t_re = y_re * tw_cos + y_im * tw_sin
    t_im = y_im * tw_cos - y_re * tw_sin
    spec = jnp.stack([t_re, t_im], axis=1)
    spec = lax.all_to_all(spec, "seq", split_axis=0, concat_axis=0, tiled=True)

    q_cos, q_sin = angle_table(dev_ids, dev_ids, devices)
    stage_a = mat_dot(jnp.concatenate([q_cos, q_sin], axis=0), spec.reshape(devices, -1))
    stage_a = stage_a.reshape(2, devices, pair, 2, n_arr, width)
    a_re = stage_a[0, :, :, 0] + stage_a[1, :, :, 1]
    a_im = stage_a[0, :, :, 1] - stage_a[1, :, :, 0]
    mid_cos, mid_sin = angle_table(dev_ids, lane_blk, seg_len)
    mid_cos = mid_cos[:, None, None, :]
    mid_sin = mid_sin[:, None, None, :]
    b_re = (a_re * mid_cos + a_im * mid_sin).reshape(devices, pair, n_arr, block_w, channels)
    b_im = (a_im * mid_cos - a_re * mid_sin).reshape(devices, pair, n_arr, block_w, channels)
    m_cos, m_sin = angle_table(blk_ids, blk_ids, block_w)

    def blk_mix(table, vals):
        return jnp.einsum(
            "mb,qkzbc->qkzmc", table, vals, preferred_element_type=jnp.float32,
            precision=exact_mode,
        )

    s_re = blk_mix(m_cos, b_re) + blk_mix(m_sin, b_im)
    s_im = blk_mix(m_cos, b_im) - blk_mix(m_sin, b_re)

    sig_r, cot_r, tap_r = s_re[:, :, 0], s_re[:, :, 1], s_re[:, :, 2]
    sig_i, cot_i, tap_i = s_im[:, :, 0], s_im[:, :, 1], s_im[:, :, 2]
    prod_r = jnp.stack(
        [sig_r * tap_r - sig_i * tap_i, cot_r * tap_r + cot_i * tap_i, cot_r * sig_r + cot_i * sig_i],
        axis=2,
    )
    prod_i = jnp.stack(
        [sig_r * tap_i + sig_i * tap_r, cot_i * tap_r - cot_r * tap_i, cot_i * sig_r - cot_r * sig_i],
        axis=2,
    )

    u_re = blk_mix(m_cos, prod_r) - blk_mix(m_sin, prod_i)
    u_im = blk_mix(m_cos, prod_i) + blk_mix(m_sin, prod_r)
    u_re = u_re.reshape(devices, pair, n_arr, width)
    u_im = u_im.reshape(devices, pair, n_arr, width)
    v_re = u_re * mid_cos - u_im * mid_sin
    v_im = u_im * mid_cos + u_re * mid_sin
    v_all = jnp.stack([v_re, v_im]).reshape(2 * devices, -1)
    inv_mat = jnp.concatenate(
        [
            jnp.concatenate([q_cos, -q_sin], axis=1),
            jnp.concatenate([q_sin, q_cos], axis=1),
        ],
        axis=0,
    )
    w_all = mat_dot(inv_mat, v_all).reshape(2, devices, pair, n_arr, width)
    b_rows = dev_ids[:, None] * block_w + lane_blk[None, :]
    k1_own = rank_seq * pair + jnp.arange(pair, dtype=jnp.int32)
    ex_ang = (b_rows[:, None, :] * k1_own[None, :, None]) % fft_size
    ex_ang = ex_ang.astype(jnp.float32) * (2.0 * math.pi / fft_size)
    ex_cos = jnp.cos(ex_ang)[:, :, None, :]
    ex_sin = jnp.sin(ex_ang)[:, :, None, :]
    x_re = w_all[0] * ex_cos - w_all[1] * ex_sin
    x_im = w_all[0] * ex_sin + w_all[1] * ex_cos
    back = jnp.stack([x_re, x_im], axis=1)
    back = lax.all_to_all(back, "seq", split_axis=0, concat_axis=0, tiled=True)

    back = back.reshape(devices, 2, pair, n_arr * width)
    back = jnp.transpose(back, (1, 0, 2, 3)).reshape(2 * rows_all, n_arr * width)
    out_mat = jnp.concatenate([col_cos.T, -col_sin.T], axis=1)
    res = (mat_dot(out_mat, back) * inv_scale).reshape(devices, n_arr, width)

    rows_out = lax.all_to_all(
        res[:, 0:2].astype(jnp.bfloat16), "seq", split_axis=0, concat_axis=0, tiled=True
    )
    conv_out = rows_out[:, 0].reshape(1, seg_len // 2, 2 * channels)
    d_signal = rows_out[:, 1].reshape(1, seg_len // 2, 2 * channels)

    d_taps = res[:, 2].reshape(devices * block_w, channels)
    d_raw = d_taps * envelope
    d_preact = mat_dot(d_raw, w_out.T) * jnp.cos(preact)
    out_part = mat_dot(hidden.T, d_raw)
    embed_part = mat_dot(features.T, d_preact)
    bias_part = jnp.sum(d_preact, axis=0)
    out_sum = lax.psum(out_part, "seq")
    embed_all, bias_all = lax.psum((embed_part, bias_part), ("seq", "chan"))
    norm_scale = 1.0 / math.sqrt(seq_total)
    return (conv_out, d_signal, embed_all * norm_scale, bias_all * norm_scale, out_sum * norm_scale)


def solution(mesh):
    return jax.shard_map(
        local,
        mesh=mesh,
        in_specs=(
            P("chan", "seq", None),
            P("chan", "seq", None),
            P(),
            P(),
            P(),
            P(None, "chan"),
            P("chan"),
        ),
        out_specs=(P("chan", "seq", None), P("chan", "seq", None), P(), P(), P(None, "chan")),
        check_vma=False,
    )
```

time: 1690 us -> 627 us (0.37)
  local copies, waits for them, and re-layouts: 1130 us -> 80.4 us
  starting transfers between devices: 88.6 us -> 29.3 us
  blocking collectives: 288 us -> 345 us
  matrix products: 88.8 us -> 58.9 us
  waiting for transfers between devices: 44.2 us -> 64.5 us
    unnamed x52 -> x32, local copies, waits for them, and re-layouts: 683 us -> 0.68 us
    all_to_all x8 -> x2, local copies, waits for them, and re-layouts: 217 us -> 7.27 us  [the longest x1 3.72 us: local(): spec = lax.all_to_all(spec, 'seq', split_axis=0, concat_axis=0, tiled=True)]
    another operation x9, local copies, waits for them, and re-layouts: 181 us -> 17 us  [the longest x1 4.67 us: local(): back = jnp.stack([x_re, x_im], axis=1)]
    all_to_all x12 -> x4, starting transfers between devices: 88.6 us -> 29.3 us  [the longest x1 9.88 us: local(): cols = lax.all_to_all(src, 'seq', split_axis=0, concat_axis=0, tiled=True)]
    psum x2, blocking collectives: 288 us -> 345 us  [the longest x1 281 us: local(): out_sum = lax.psum(out_part, 'seq')]
    dot_general x48 -> x8, matrix products: 74.2 us -> 32.6 us  [blk_mix(): jnp.einsum('mb,qkzbc->qkzmc', table, vals, preferred_element_type=jnp.flo...]
    all_to_all x12 -> x4, waiting for transfers between devices: 44.2 us -> 64.5 us  [the longest x1 38.9 us: local(): back = lax.all_to_all(back, 'seq', split_axis=0, concat_axis=0, tiled=True)]
  transfers between devices with their start and end apart: 12 -> 4, of which waited for: 6 -> 3; matrix products, arithmetic and copies ran while one was open for 59% -> 4% of each run, Pallas kernels for 0% -> 0%
where the time goes in v1:
time: 627 us; the launch traced here: 616 us
  blocking collectives  345 us (55%)
  local copies, waits for them, and re-layouts  80.4 us (13%)
  waiting for transfers between devices  64.5 us (10%)
  matrix products  58.9 us (9%)
  other arithmetic  35.8 us (6%)
  starting transfers between devices  29.3 us (5%)
    psum x1, blocking collectives, local(): out_sum = lax.psum(out_part, 'seq')  281 us
    psum x1, blocking collectives, local(): embed_all, bias_all = lax.psum((embed_part, bias_part), ('seq', 'chan'))  64.6 us
    all_to_all x1, waiting for transfers between devices, local(): back = lax.all_to_all(back, 'seq', split_axis=0, concat_axis=0, tiled=True)  38.9 us
    dot_general x8, matrix products, blk_mix(): jnp.einsum('mb,qkzbc->qkzmc', table, vals, preferred_element_type=jnp.flo...  32.6 us
    dot_general x10, matrix products, mat_dot(): jnp.dot(lhs_mat, rhs_mat, preferred_element_type=jnp.float32, precision=e...  26.2 us
    all_to_all x1, waiting for transfers between devices, local(): spec = lax.all_to_all(spec, 'seq', split_axis=0, concat_axis=0, tiled=True)  23.2 us
  transfers between devices with their start and end apart: 4, of which 3 were waited for; matrix products, arithmetic and copies ran while one was open for 4% of the time, Pallas kernels for 0%

profile of v1, /device:TPU:0, one launch (start us, length us, event | category | flops | bytes accessed | tf_op | source)
XLA Modules:
  0.0 615.8 jit_solution(7838954913175535610)
XLA Ops:
  0.6 1.2 stack_reshape.8
  1.9 1.2 stack_reshape.9
  3.1 1.3 pad_maximum_fusion.14
  4.4 9.9 %all-to-all-start = ((bf16[64,2,1024]{2,1,0:T(2,128)(2,1)}), bf16[64,2,1024]{2,1,0:T(2,128)(2,1)S(1)}, u32[]{:S(2)}, u32[]{:S(2)}) async-start(bf16[64,2,1024]{2,1,0:T(2,128)(2,1)} %pad_maximum_fusion.14), calls=%async_computation | async-start | bytes 524288 | tf_op jit(solution)/shard_map/all_to_all | solution.py:65
  14.5 0.7 fusion.180
  15.2 1.0 fusion.84
  16.2 2.7 fusion.181
  19.9 2.0 fusion.35
  21.9 2.3 all-to-all-done
  24.9 1.9 convolution_negate_fusion
  26.8 2.3 add_bitcast_fusion.2
  29.3 4.1 copy.76
  33.4 6.9 %all-to-all-start.1 = ((f32[128,2,3,1024]{3,1,2,0:T(2,128)}), f32[128,2,3,1024]{3,1,2,0:T(2,128)S(1)}, u32[]{:S(2)}, u32[]{:S(2)}) async-start(f32[128,2,3,1024]{3,1,2,0:T(2,128)} %copy.76), calls=%async_computation.1 | async-start | bytes 6291456 | tf_op jit(solution)/shard_map/all_to_all | solution.py:86
  40.3 0.8 fusion.100
  42.6 1.8 fusion.44
  44.4 2.9 fusion.33
  47.2 9.5 %fusion.38 = (f32[64,2,1024]{2,1,0:T(2,128)}, f32[64,2,1024]{2,1,0:T(2,128)}) fusion(s32[2]{0:T(128)S(1)} %iota_add_fusion.1, s32[64,1024]{1,0:T(8,128)S(1)} %broadcast_add_fusion), kind=kLoop, calls=%fused_computation.88 | loop fusion | flops 1835008 | bytes 1310728 | tf_op jit(solution)/shard_map/cos | solution.py:139
  56.8 23.2 %all-to-all-done.1 = f32[128,2,3,1024]{3,1,2,0:T(2,128)S(1)} async-done(((f32[128,2,3,1024]{3,1,2,0:T(2,128)}), f32[128,2,3,1024]{3,1,2,0:T(2,128)S(1)}, u32[]{:S(2)}, u32[]{:S(2)}) %all-to-all-start.1) | async-done | bytes 3145760 | tf_op jit(solution)/shard_map/all_to_all | solution.py:86
  80.0 3.7 copy.77
  83.7 4.3 reshape.397
  88.0 3.7 dot_general.72
  91.8 9.4 %fusion = f32[2,64,2,2,3,1024]{5,1,4,3,2,0:T(8,128)S(1)} fusion(f32[2,64,64,1,1,1]{2,1,5,4,3,0:T(8,128)} %bitcast.98, f32[2,2,3,1024,64]{3,2,1,0,4:T(4,128)} %dot_general.72), kind=kOutput, calls=%fused_computation.6 | convolution fusion | flops 1207959552 | bytes 9469952 | tf_op jit(solution)/shard_map/dot_general | solution.py:12
  101.2 2.7 slice_add_fusion
  103.8 2.5 add.319
  106.4 3.6 sub.92
  110.0 5.5 fusion.51
  115.5 3.3 fusion.52
  118.8 3.3 add_bitcast_fusion.1
  122.1 3.5 subtract_bitcast_fusion.1
  126.2 0.7 multiply_subtract_fusion.5
  126.9 3.0 fusion.4
  130.0 2.9 fusion.3
  132.9 4.7 subtract_bitcast_fusion
  137.6 4.9 reshape.411
  142.5 6.4 %add_bitcast_fusion = f32[64,2,3,16,64]{4,3,2,1,0:T(8,128)} fusion(f32[64,2,3,64,16]{3,4,2,1,0:T(8,128)S(1)} %fusion.3, f32[64,2,1,16,64]{4,3,2,1,0:T(8,128)} %copy-done.5, f32[64,2,1,16,64]{4,3,2,1,0:T(8,128)} %copy-done.6, f32[64,2,1,16,64]{4,3,2,1,0:T(8,128)} %copy-done.4), kind=kOutput, calls=%fused_computation.9 | convolution fusion | flops 76680704 | bytes 4718592 | tf_op jit(solution)/shard_map/mb,qkzbc->qkzmc/dot_general | solution.py:101
  148.9 4.6 reshape.412
  153.6 3.3 multiply_subtract_fusion.2
  157.1 4.1 copy.85
  161.2 5.0 reshape.400
  166.2 3.8 fusion.63
  170.0 1.8 fusion.179
  171.9 3.1 squeeze.4
  174.9 3.9 squeeze.5
  178.9 2.4 multiply_subtract_fusion.1
  181.3 1.6 pad_maximum_fusion
  182.9 4.7 copy.86
  187.5 6.6 %all-to-all-start.2 = ((f32[64,2,2,3,1024]{4,2,3,1,0:T(2,128)}), f32[64,2,2,3,1024]{4,2,3,1,0:T(2,128)S(1)}, u32[]{:S(2)}, u32[]{:S(2)}) async-start(f32[64,2,2,3,1024]{4,2,3,1,0:T(2,128)} %copy.86), calls=%async_computation.2 | async-start | bytes 6291456 | tf_op jit(solution)/shard_map/all_to_all | solution.py:144
  194.1 0.8 sine_negate_fusion
  194.9 38.9 %all-to-all-done.2 = f32[64,2,2,3,1024]{4,2,3,1,0:T(2,128)S(1)} async-done(((f32[64,2,2,3,1024]{4,2,3,1,0:T(2,128)}), f32[64,2,2,3,1024]{4,2,3,1,0:T(2,128)S(1)}, u32[]{:S(2)}, u32[]{:S(2)}) %all-to-all-start.2) | async-done | bytes 3145760 | tf_op jit(solution)/shard_map/all_to_all | solution.py:144
  233.8 3.6 copy.87
  237.4 5.0 reshape.401
  242.3 4.1 copy.88
  246.4 3.9 reshape.402
  250.3 3.7 convolution_multiply_fusion
  254.0 1.7 reshape.403
  255.7 0.7 slice_reduce_fusion
  256.5 0.9 slice.117
  258.2 1.3 fusion.182
  259.9 64.6 %all-reduce = (f32[32,64]{1,0:T(8,128)S(1)}, f32[64]{0:T(128)S(1)}) all-reduce(f32[32,64]{1,0:T(8,128)S(1)} %fusion.53, f32[64]{0:T(128)S(1)} %get-tuple-element.41), channel_id=1, replica_groups=mesh['seq'=64,'chan'=2] {'seq','chan'}, use_global_device_ids=true, to_apply=%region_0.1 | all-reduce | flops 2112 | bytes 16896 | tf_op jit(solution)/shard_map/psum | solution.py:164
  325.1 5.9 all-to-all-start.3
  331.5 280.7 %psum.23 = f32[64,64]{1,0:T(8,128)S(1)} all-reduce(f32[64,64]{1,0:T(8,128)S(1)} %fusion.40), channel_id=1, replica_groups=mesh['seq'=64,'chan'=2] {'seq'}, use_global_device_ids=true, to_apply=%region_3.4 | all-reduce | flops 4096 | bytes 32768 | tf_op jit(solution)/shard_map/psum | solution.py:163
  612.8 1.1 slice_reduce_fusion.1
  613.9 0.7 reshape_squeeze.10
  614.6 0.7 reshape_squeeze.9
  (61 shorter events, 7.2 us)
Async XLA Ops:
  0.6 18.3 %copy-start = (f32[64,64]{1,0:T(8,128)S(1)}, f32[64,64]{1,0:T(8,128)}, u32[]{:S(2)}) copy-start(f32[64,64]{1,0:T(8,128)} %param.12) | copy-start | bytes 49156
  4.4 19.8 %all-to-all-start = ((bf16[64,2,1024]{2,1,0:T(2,128)(2,1)}), bf16[64,2,1024]{2,1,0:T(2,128)(2,1)S(1)}, u32[]{:S(2)}, u32[]{:S(2)}) async-start(bf16[64,2,1024]{2,1,0:T(2,128)(2,1)} %pad_maximum_fusion.14), calls=%async_computation | async-start | bytes 524288 | tf_op jit(solution)/shard_map/all_to_all | solution.py:65
  16.2 2.7 copy-start.13
  33.4 46.6 %all-to-all-start.1 = ((f32[128,2,3,1024]{3,1,2,0:T(2,128)}), f32[128,2,3,1024]{3,1,2,0:T(2,128)S(1)}, u32[]{:S(2)}, u32[]{:S(2)}) async-start(f32[128,2,3,1024]{3,1,2,0:T(2,128)} %copy.76), calls=%async_computation.1 | async-start | bytes 6291456 | tf_op jit(solution)/shard_map/all_to_all | solution.py:86
  41.2 0.6 copy-start.15
  109.9 5.5 copy-start.1
  110.0 5.5 copy-start.2
  110.0 5.5 copy-start.3
  126.2 6.8 %copy-start.6 = (f32[64,2,1,16,64]{4,3,2,1,0:T(8,128)}, f32[64,2,1,16,64]{4,3,2,1,0:T(8,128)S(1)}, u32[]{:S(2)}) copy-start(f32[64,2,1,16,64]{4,3,2,1,0:T(8,128)S(1)} %get-tuple-element.13) | copy-start | bytes 1572868
  126.9 6.0 copy-start.4
  126.9 6.0 copy-start.5
  148.9 4.6 copy-start.7
  148.9 4.6 copy-start.10
  148.9 4.6 copy-start.11
  171.9 7.0 %copy-start.8 = (f32[64,2,1024]{2,1,0:T(2,128)S(1)}, f32[64,2,1024]{2,1,0:T(2,128)}, u32[]{:S(2)}) copy-start(f32[64,2,1024]{2,1,0:T(2,128)} %get-tuple-element.25) | copy-start | bytes 1572868
  171.9 7.0 %copy-start.9 = (f32[64,2,1024]{2,1,0:T(2,128)S(1)}, f32[64,2,1024]{2,1,0:T(2,128)}, u32[]{:S(2)}) copy-start(f32[64,2,1024]{2,1,0:T(2,128)} %get-tuple-element.26) | copy-start | bytes 1572868
  187.5 46.3 %all-to-all-start.2 = ((f32[64,2,2,3,1024]{4,2,3,1,0:T(2,128)}), f32[64,2,2,3,1024]{4,2,3,1,0:T(2,128)S(1)}, u32[]{:S(2)}, u32[]{:S(2)}) async-start(f32[64,2,2,3,1024]{4,2,3,1,0:T(2,128)} %copy.86), calls=%async_computation.2 | async-start | bytes 6291456 | tf_op jit(solution)/shard_map/all_to_all | solution.py:144
  254.0 4.2 copy-start.12
  254.0 5.6 copy-start.14
  325.1 287.8 %all-to-all-start.3 = ((bf16[64,2,1024]{2,1,0:T(2,128)(2,1)}), bf16[64,2,1024]{2,1,0:T(2,128)(2,1)S(1)}, u32[]{:S(2)}, u32[]{:S(2)}) async-start(bf16[64,2,1024]{2,1,0:T(2,128)(2,1)} %slice.117), calls=%async_computation.3 | async-start | bytes 524288 | tf_op jit(solution)/shard_map/all_to_all | solution.py:151
